TPU v7x, 32 devices: a whole 2x2x4 slice. The times are simulated.
32 devices in a mesh: cap: 4 (over z), lat: 4 (over x, core), rad: 2 (over y).
Axes of the slice: x: 2, y: 2, z: 4, core: 2. Of those that a mesh axis runs over, the one named last changes fastest.
Arguments:
- adjoint_temp: float32 [64, 128, 1024], P('rad', 'cap', 'lat'), may hold values from -6 to 6
- velocity: bfloat16 [2, 64, 128, 1024], P(None, 'rad', 'cap', 'lat'), may hold values from -6 to 6
- visc_flow: bfloat16 [64, 128, 1024], P('rad', 'cap', 'lat'), may hold values from 0.099609375 to 1
- visc_yield: bfloat16 [64, 128, 1024], P('rad', 'cap', 'lat'), may hold values from 0.049804688 to 1
- yield_mask: int32 [64, 128, 1024], P('rad', 'cap', 'lat'), may hold values 0 or 1
- radial_inverse: float32 [64, 64], replicated
- marker_rows: bfloat16 [64, 32768], P('rad', ('cap', 'lat')), may hold values from -6 to 6
- recv_cells: int32 [32768], P(('cap', 'lat')), may hold values from 0 to 8191
- recv_counts: int32 [64], P(('cap', 'lat')), may hold values from 64 to 512, as said below
Outputs:
- adjoint_prev: float32 [64, 128, 1024], P(None, ('cap', 'rad'), 'lat')
Inputs may be any that keep to these rules, and one draw needn't show every extreme that they name: `recv_counts`: some bucket holds exactly 512 live slots and some exactly 64 in every draw.
All inputs are finite; a program needn't handle non-finite values. No bound on the sum of `yield_mask` on one device may be relied on, other than what follows from the above.
Results may differ from a plain program's by a relative error of at most 0.0003.
Values may be sent and summed in bfloat16 or wider, within the bound.
No kernel may reach another device: no remote copies, remote signals or barrier semaphores. Data moves between devices by JAX's collectives and lax.ppermute only.
A program may use at most 64 MiB of HBM per device.

v0:
```python
import math
import jax
import jax.numpy as jnp
from jax import lax
from jax.sharding import PartitionSpec as P

PICARD = 3
relax_coef = 0.25
advect_coef = 0.1


def extended(x, sides, width):
    for axis, dim in sides:
        devices, length = (lax.axis_size(axis), x.shape[dim])
        up = [(i, (i + 1) % devices) for i in range(devices - 1)]
        down = [(j, i) for i, j in up]
        last = lax.slice_in_dim(x, length - width, length, axis=dim)
        first = lax.slice_in_dim(x, 0, width, axis=dim)
        before = lax.ppermute(last, axis, up)
        after = lax.ppermute(first, axis, down)
        x = jnp.concatenate([before, x, after], axis=dim)
    return x


def viscous(w_pad, eta_pad, w_mid, eta_mid):
    total = jnp.zeros_like(w_mid)
    for neigh_w, neigh_e in (
        (w_pad[:, 2:, 1:-1], eta_pad[:, 2:, 1:-1]),
        (w_pad[:, :-2, 1:-1], eta_pad[:, :-2, 1:-1]),
        (w_pad[:, 1:-1, 2:], eta_pad[:, 1:-1, 2:]),
        (w_pad[:, 1:-1, :-2], eta_pad[:, 1:-1, :-2]),
    ):
        total = total + 0.5 * (eta_mid + neigh_e) * (neigh_w - w_mid)
    return total


def per_device(
    adjoint_temp,
    velocity,
    visc_flow,
    visc_yield,
    yield_mask,
    radial_inverse,
    marker_rows,
    recv_cells,
    recv_counts,
):
    layers, first_len, second_len = adjoint_temp.shape
    flow = visc_flow.astype(jnp.float32)
    plast = visc_yield.astype(jnp.float32)
    eta = jnp.where(yield_mask == 1, flow * plast / (flow + plast), flow)
    iterate = adjoint_temp
    lam_pad = None
    for sweep in range(PICARD):
        padded = extended(jnp.stack([iterate, eta]), (("cap", 2), ("lat", 3)), 1)
        if sweep == 0:
            lam_pad = padded[0]
        iterate = adjoint_temp + relax_coef * viscous(padded[0], padded[1], iterate, eta)
    advect = velocity[0] * (lam_pad[:, 2:, 1:-1] - lam_pad[:, :-2, 1:-1]) + velocity[1] * (
        lam_pad[:, 1:-1, 2:] - lam_pad[:, 1:-1, :-2]
    )
    received = lax.all_to_all(marker_rows, "lat", split_axis=1, concat_axis=1, tiled=True)
    senders = lax.axis_size("lat")
    slot_total = received.shape[1]
    per_sender = slot_total // senders
    live = (jnp.arange(per_sender, dtype=jnp.int32)[None, :] < recv_counts[:, None]).reshape(-1)
    target = jnp.where(live, recv_cells, -1)
    block = math.gcd(slot_total, 512)
    blocks = slot_total // block
    cell_count = first_len * second_len
    rows_blocks = received.reshape(layers, blocks, block).transpose(1, 0, 2)
    target_blocks = target.reshape(blocks, block)
    cell_ids = jnp.arange(cell_count, dtype=jnp.int32)

    def deposit_block(total, item):
        rows_part, target_part = item
        onehot = (target_part[:, None] == cell_ids[None, :]).astype(jnp.bfloat16)
        return (total + jnp.dot(rows_part, onehot, preferred_element_type=jnp.float32), None)

    deposit, unused = lax.scan(
        deposit_block, jnp.zeros((layers, cell_count), jnp.float32), (rows_blocks, target_blocks)
    )
    deposit = deposit.reshape(layers, first_len, second_len)
    rhs = iterate + advect_coef * advect + deposit
    full_layers = radial_inverse.shape[0]
    columns = lax.all_to_all(rhs, "rad", split_axis=1, concat_axis=0, tiled=True)
    result = jnp.dot(
        radial_inverse, columns.reshape(full_layers, -1), precision=lax.Precision.HIGHEST
    )
    return result.reshape(columns.shape)


def solution(mesh):
    in_specs = (
        P("rad", "cap", "lat"),
        P(None, "rad", "cap", "lat"),
        P("rad", "cap", "lat"),
        P("rad", "cap", "lat"),
        P("rad", "cap", "lat"),
        P(),
        P("rad", ("cap", "lat")),
        P(("cap", "lat")),
        P(("cap", "lat")),
    )
    out_specs = P(None, ("cap", "rad"), "lat")
    return jax.shard_map(
        per_device, mesh=mesh, in_specs=in_specs, out_specs=out_specs, check_vma=False
    )
```

profile of v0, /device:TPU:1, one launch (start us, length us, event | category | flops | bytes accessed | tf_op | source)
XLA Modules:
  0.0 151.4 jit_solution(331933865882135294)
XLA Ops:
  0.0 1.9 %convert_select_fusion = f32[32,32,256]{2,1,0:T(8,128)S(1)} fusion(bf16[32,32,256]{2,1,0:T(8,128)(2,1)} %param.13, bf16[32,32,256]{2,1,0:T(8,128)(2,1)} %param.14, s32[32,32,256]{2,1,0:T(8,128)} %param.15), kind=kLoop, calls=%fused_computation.43 | loop fusion | flops 1835008 | bytes 3145728 | tf_op jit(solution)/shard_map/jit(_where)/select_n | solution.py:51
  2.1 4.0 %collective-permute-start = (f32[2,32,1,256]{3,2,1,0:T(1,128)S(1)}, f32[2,32,1,256]{3,2,1,0:T(1,128)S(1)}, u32[]{:S(2)}, u32[]{:S(2)}) collective-permute-start(f32[2,32,1,256]{3,2,1,0:T(1,128)S(1)} %get-tuple-element.62), channel_id=1, source_target_pairs={{0,8},{8,16},{16,24},{1,9},{9,17},{17,25},{2,10},{10,18},{18,26},{... | collective-permute-start | bytes 196616 | tf_op jit(solution)/shard_map/ppermute | solution.py:19
  6.1 1.3 collective-permute-start.1
  7.4 3.7 %collective-permute-done.1 = f32[2,32,1,256]{3,2,1,0:T(1,128)S(1)} collective-permute-done((f32[2,32,1,256]{3,2,1,0:T(1,128)S(1)}, f32[2,32,1,256]{3,2,1,0:T(1,128)S(1)}, u32[]{:S(2)}, u32[]{:S(2)}) %collective-permute-start.1) | collective-permute-done | bytes 65568 | tf_op jit(solution)/shard_map/ppermute | solution.py:20
  11.1 0.4 fusion.21
  11.6 1.9 %fusion.75 = (f32[2,32,34,1]{3,2,1,0:T(8,128)}, f32[2,32,34,1]{3,2,1,0:T(8,128)}) fusion(f32[2,32,34,256]{3,2,1,0:T(8,128)S(1)} %fusion.21), kind=kLoop, calls=%fused_computation.124 | loop fusion | bytes 34816 | tf_op jit(solution)/shard_map/slice | solution.py:17
  13.5 1.9 %copy.28 = f32[2,32,34,1]{2,1,3,0:T(8,128)S(1)} copy(f32[2,32,34,1]{3,2,1,0:T(8,128)} %get-tuple-element.76) | data formatting | bytes 17408 | tf_op jit(solution)/shard_map/slice | solution.py:17
  15.3 5.1 %collective-permute-start.2 = (f32[2,32,34,1]{2,1,3,0:T(8,128)S(1)}, f32[2,32,34,1]{2,1,3,0:T(8,128)S(1)}, u32[]{:S(2)}, u32[]{:S(2)}) collective-permute-start(f32[2,32,34,1]{2,1,3,0:T(8,128)S(1)} %copy.28), channel_id=1, source_target_pairs={{0,2},{2,4},{4,6},{1,3},{3,5},{5,7},{8,10},{10,12},{12,14},{9,11},... | collective-permute-start | bytes 26120 | tf_op jit(solution)/shard_map/ppermute | solution.py:19
  20.4 1.9 %copy.29 = f32[2,32,34,1]{2,1,3,0:T(8,128)S(1)} copy(f32[2,32,34,1]{3,2,1,0:T(8,128)} %get-tuple-element.77) | data formatting | bytes 17408 | tf_op jit(solution)/shard_map/slice | solution.py:18
  22.3 1.9 %collective-permute-start.3 = (f32[2,32,34,1]{2,1,3,0:T(8,128)S(1)}, f32[2,32,34,1]{2,1,3,0:T(8,128)S(1)}, u32[]{:S(2)}, u32[]{:S(2)}) collective-permute-start(f32[2,32,34,1]{2,1,3,0:T(8,128)S(1)} %copy.29), channel_id=1, source_target_pairs={{2,0},{4,2},{6,4},{3,1},{5,3},{7,5},{10,8},{12,10},{14,12},{11,9},... | collective-permute-start | bytes 26120 | tf_op jit(solution)/shard_map/ppermute | solution.py:20
  24.2 1.6 %copy.30 = f32[2,32,34,1]{3,2,1,0:T(8,128)} copy(f32[2,32,34,1]{2,1,3,0:T(8,128)S(1)} %collective-permute-done.2) | data formatting | bytes 17408 | tf_op jit(solution)/shard_map/ppermute | solution.py:19
  25.9 1.7 %collective-permute-done.3 = f32[2,32,34,1]{2,1,3,0:T(8,128)S(1)} collective-permute-done((f32[2,32,34,1]{2,1,3,0:T(8,128)S(1)}, f32[2,32,34,1]{2,1,3,0:T(8,128)S(1)}, u32[]{:S(2)}, u32[]{:S(2)}) %collective-permute-start.3) | collective-permute-done | bytes 8736 | tf_op jit(solution)/shard_map/ppermute | solution.py:20
  27.5 1.6 %copy.31 = f32[2,32,34,1]{3,2,1,0:T(8,128)} copy(f32[2,32,34,1]{2,1,3,0:T(8,128)S(1)} %collective-permute-done.3) | data formatting | bytes 17408 | tf_op jit(solution)/shard_map/ppermute | solution.py:20
  29.2 4.3 %fusion.11 = f32[2,32,34,258]{3,2,1,0:T(8,128)S(1)} fusion(f32[1,32,32,256]{3,2,1,0:T(8,128)S(1)} %bitcast.53, f32[2,32,34,1]{3,2,1,0:T(8,128)} %copy.31, f32[2,32,1,256]{3,2,1,0:T(1,128)S(1)} %collective-permute-done.1, f32[1,32,32,256]{3,2,1,0:T(8,128)S(1)} %bitcast.60, f32[2,32,1,256]{3,2,1,0:T(1,128)S(1)} %collective-permute-done, f32[2,32,34,1]{3,2,1,0:T(8,128)} %copy.30), kind=kLoop, calls=%fused_computation.15 | loop fusion | flops 2807040 | bytes 4491264 | tf_op jit(solution)/shard_map/concatenate | solution.py:21
  33.7 1.0 copy-done.2
  34.7 2.0 %fusion.58 = f32[32,32,256]{2,1,0:T(8,128)S(1)} fusion(f32[32,32,256]{2,1,0:T(8,128)S(1)} %copy-done.2, f32[32,32,256]{2,1,0:T(8,128)S(1)} %convert_select_fusion, f32[32,34,258]{2,1,0:T(8,128)S(1)} %get-tuple-element.71, f32[32,34,258]{2,1,0:T(8,128)S(1)} %get-tuple-element.70), kind=kLoop, calls=%fused_computation.96 | loop fusion | flops 5505024 | bytes 11534336 | tf_op jit(solution)/shard_map/add | solution.py:58
  36.7 1.0 copy-done.7
  37.6 0.7 fusion.70
  38.4 3.2 %collective-permute-start.4 = (f32[2,32,1,256]{3,2,1,0:T(1,128)}, f32[2,32,1,256]{3,2,1,0:T(1,128)S(1)}, u32[]{:S(2)}, u32[]{:S(2)}) collective-permute-start(f32[2,32,1,256]{3,2,1,0:T(1,128)} %get-tuple-element.80), channel_id=1, source_target_pairs={{0,8},{8,16},{16,24},{1,9},{9,17},{17,25},{2,10},{10,18},{18,26},{... | collective-permute-start | bytes 196616 | tf_op jit(solution)/shard_map/ppermute | solution.py:19
  41.6 1.3 collective-permute-start.5
  42.9 0.6 copy.49
  43.5 3.3 %all-to-all-start = ((bf16[32,4,512]{2,0,1:T(8,128)(2,1)}), bf16[32,4,512]{2,0,1:T(8,128)(2,1)S(1)}, u32[]{:S(2)}, u32[]{:S(2)}) async-start(bf16[32,4,512]{2,0,1:T(8,128)(2,1)} %bitcast.46), calls=%async_computation | async-start | bytes 262144 | tf_op jit(solution)/shard_map/all_to_all | solution.py:62
  46.9 1.6 %fusion.23 = f32[2,32,34,256]{3,2,1,0:T(8,128)S(1)} fusion(f32[1,32,32,256]{3,2,1,0:T(8,128)S(1)} %bitcast.54, f32[2,32,1,256]{3,2,1,0:T(1,128)S(1)} %collective-permute-done.5, f32[1,32,32,256]{3,2,1,0:T(8,128)} %bitcast.65, f32[2,32,1,256]{3,2,1,0:T(1,128)S(1)} %collective-permute-done.4), kind=kLoop, calls=%fused_computation.30 | loop fusion | flops 1671168 | bytes 4456448 | tf_op jit(solution)/shard_map/concatenate | solution.py:21
  48.5 1.9 %fusion.74 = (f32[2,32,34,1]{3,2,1,0:T(8,128)}, f32[2,32,34,1]{3,2,1,0:T(8,128)}) fusion(f32[2,32,34,256]{3,2,1,0:T(8,128)S(1)} %fusion.23), kind=kLoop, calls=%fused_computation.123 | loop fusion | bytes 34816 | tf_op jit(solution)/shard_map/slice | solution.py:17
  50.4 1.9 %copy.32 = f32[2,32,34,1]{2,1,3,0:T(8,128)S(1)} copy(f32[2,32,34,1]{3,2,1,0:T(8,128)} %get-tuple-element.74) | data formatting | bytes 17408 | tf_op jit(solution)/shard_map/slice | solution.py:17
  52.2 3.1 %collective-permute-start.6 = (f32[2,32,34,1]{2,1,3,0:T(8,128)S(1)}, f32[2,32,34,1]{2,1,3,0:T(8,128)S(1)}, u32[]{:S(2)}, u32[]{:S(2)}) collective-permute-start(f32[2,32,34,1]{2,1,3,0:T(8,128)S(1)} %copy.32), channel_id=1, source_target_pairs={{0,2},{2,4},{4,6},{1,3},{3,5},{5,7},{8,10},{10,12},{12,14},{9,11},... | collective-permute-start | bytes 26120 | tf_op jit(solution)/shard_map/ppermute | solution.py:19
  55.4 1.9 %copy.33 = f32[2,32,34,1]{2,1,3,0:T(8,128)S(1)} copy(f32[2,32,34,1]{3,2,1,0:T(8,128)} %get-tuple-element.75) | data formatting | bytes 17408 | tf_op jit(solution)/shard_map/slice | solution.py:18
  57.2 2.1 %collective-permute-start.7 = (f32[2,32,34,1]{2,1,3,0:T(8,128)S(1)}, f32[2,32,34,1]{2,1,3,0:T(8,128)}, u32[]{:S(2)}, u32[]{:S(2)}) collective-permute-start(f32[2,32,34,1]{2,1,3,0:T(8,128)S(1)} %copy.33), channel_id=1, source_target_pairs={{2,0},{4,2},{6,4},{3,1},{5,3},{7,5},{10,8},{12,10},{14,12},{11,9},... | collective-permute-start | bytes 26120 | tf_op jit(solution)/shard_map/ppermute | solution.py:20
  59.4 1.6 %copy.34 = f32[2,32,34,1]{3,2,1,0:T(8,128)} copy(f32[2,32,34,1]{2,1,3,0:T(8,128)S(1)} %collective-permute-done.6) | data formatting | bytes 17408 | tf_op jit(solution)/shard_map/ppermute | solution.py:19
  61.1 1.5 collective-permute-done.7
  62.5 2.4 %copy.35 = f32[2,32,34,1]{3,2,1,0:T(8,128)} copy(f32[2,32,34,1]{2,1,3,0:T(8,128)} %collective-permute-done.7) | data formatting | bytes 17408 | tf_op jit(solution)/shard_map/ppermute | solution.py:20
  64.9 4.4 %fusion.15 = f32[2,32,34,258]{3,2,1,0:T(8,128)S(1)} fusion(f32[1,32,32,256]{3,2,1,0:T(8,128)S(1)} %bitcast.55, f32[2,32,34,1]{3,2,1,0:T(8,128)} %copy.35, f32[2,32,1,256]{3,2,1,0:T(1,128)S(1)} %collective-permute-done.5, f32[1,32,32,256]{3,2,1,0:T(8,128)} %bitcast.66, f32[2,32,1,256]{3,2,1,0:T(1,128)S(1)} %collective-permute-done.4, f32[2,32,34,1]{3,2,1,0:T(8,128)} %copy.34), kind=kLoop, calls=%fused_computation.19 | loop fusion | flops 2807040 | bytes 4491264 | tf_op jit(solution)/shard_map/concatenate | solution.py:21
  69.6 0.9 copy-done.3
  70.6 0.3 copy-done.8
  70.9 1.9 %fusion.44 = f32[32,32,256]{2,1,0:T(8,128)S(1)} fusion(f32[32,32,256]{2,1,0:T(8,128)S(1)} %copy-done.3, f32[32,32,256]{2,1,0:T(8,128)S(1)} %copy-done.8, f32[32,34,258]{2,1,0:T(8,128)S(1)} %get-tuple-element.69, f32[32,32,256]{2,1,0:T(8,128)S(1)} %convert_select_fusion, f32[32,34,258]{2,1,0:T(8,128)S(1)} %get-tuple-element.68), kind=kLoop, calls=%fused_computation.74 | loop fusion | flops 5505024 | bytes 12582912 | tf_op jit(solution)/shard_map/add | solution.py:58
  72.8 1.0 copy-done.5
  73.9 3.4 %collective-permute-start.8 = (f32[2,32,1,256]{3,2,1,0:T(1,128)S(1)}, f32[2,32,1,256]{3,2,1,0:T(1,128)S(1)}, u32[]{:S(2)}, u32[]{:S(2)}) collective-permute-start(f32[2,32,1,256]{3,2,1,0:T(1,128)S(1)} %get-tuple-element.78), channel_id=1, source_target_pairs={{0,8},{8,16},{16,24},{1,9},{9,17},{17,25},{2,10},{10,18},{18,26},{... | collective-permute-start | bytes 196616 | tf_op jit(solution)/shard_map/ppermute | solution.py:19
  77.3 1.3 collective-permute-start.9
  78.7 3.7 %collective-permute-done.9 = f32[2,32,1,256]{3,2,1,0:T(1,128)S(1)} collective-permute-done((f32[2,32,1,256]{3,2,1,0:T(1,128)S(1)}, f32[2,32,1,256]{3,2,1,0:T(1,128)S(1)}, u32[]{:S(2)}, u32[]{:S(2)}) %collective-permute-start.9) | collective-permute-done | bytes 65568 | tf_op jit(solution)/shard_map/ppermute | solution.py:20
  82.3 1.6 %fusion.25 = f32[2,32,34,256]{3,2,1,0:T(8,128)S(1)} fusion(f32[1,32,32,256]{3,2,1,0:T(8,128)S(1)} %bitcast.56, f32[2,32,1,256]{3,2,1,0:T(1,128)S(1)} %collective-permute-done.9, f32[1,32,32,256]{3,2,1,0:T(8,128)} %bitcast.62, f32[2,32,1,256]{3,2,1,0:T(1,128)S(1)} %collective-permute-done.8), kind=kLoop, calls=%fused_computation.32 | loop fusion | flops 1671168 | bytes 4456448 | tf_op jit(solution)/shard_map/concatenate | solution.py:21
  83.9 1.9 %fusion.73 = (f32[2,32,34,1]{3,2,1,0:T(8,128)}, f32[2,32,34,1]{3,2,1,0:T(8,128)}) fusion(f32[2,32,34,256]{3,2,1,0:T(8,128)S(1)} %fusion.25), kind=kLoop, calls=%fused_computation.122 | loop fusion | bytes 34816 | tf_op jit(solution)/shard_map/slice | solution.py:17
  85.8 1.9 %copy.36 = f32[2,32,34,1]{2,1,3,0:T(8,128)S(1)} copy(f32[2,32,34,1]{3,2,1,0:T(8,128)} %get-tuple-element.72) | data formatting | bytes 17408 | tf_op jit(solution)/shard_map/slice | solution.py:17
  87.7 3.6 %collective-permute-start.10 = (f32[2,32,34,1]{2,1,3,0:T(8,128)S(1)}, f32[2,32,34,1]{2,1,3,0:T(8,128)S(1)}, u32[]{:S(2)}, u32[]{:S(2)}) collective-permute-start(f32[2,32,34,1]{2,1,3,0:T(8,128)S(1)} %copy.36), channel_id=1, source_target_pairs={{0,2},{2,4},{4,6},{1,3},{3,5},{5,7},{8,10},{10,12},{12,14},{9,11},... | collective-permute-start | bytes 26120 | tf_op jit(solution)/shard_map/ppermute | solution.py:19
  91.3 1.9 %copy.37 = f32[2,32,34,1]{2,1,3,0:T(8,128)S(1)} copy(f32[2,32,34,1]{3,2,1,0:T(8,128)} %get-tuple-element.73) | data formatting | bytes 17408 | tf_op jit(solution)/shard_map/slice | solution.py:18
  93.1 2.1 %collective-permute-start.11 = (f32[2,32,34,1]{2,1,3,0:T(8,128)S(1)}, f32[2,32,34,1]{2,1,3,0:T(8,128)S(1)}, u32[]{:S(2)}, u32[]{:S(2)}) collective-permute-start(f32[2,32,34,1]{2,1,3,0:T(8,128)S(1)} %copy.37), channel_id=1, source_target_pairs={{2,0},{4,2},{6,4},{3,1},{5,3},{7,5},{10,8},{12,10},{14,12},{11,9},... | collective-permute-start | bytes 26120 | tf_op jit(solution)/shard_map/ppermute | solution.py:20
  95.3 21.3 %while.11 = (s32[]{:T(128)}, f32[32,8192]{1,0:T(8,128)}, bf16[4,32,512]{2,1,0:T(8,128)(2,1)S(1)}, s32[4,512]{1,0:T(4,128)S(1)}, s32[]{:T(128)}, /*index=5*/s32[]{:T(128)}) while((s32[]{:T(128)}, f32[32,8192]{1,0:T(8,128)}, bf16[4,32,512]{2,1,0:T(8,128)(2,1)S(1)}, s32[4,512]{1,0:T(4,128)S(1)}, s32[]{:T(128)}, ...), condition=%wide.region_1.2_spmd.clone, body=%wide.region_0.1_spmd.clone.sunk | while | flops 273154048 | bytes 2136151 | solution.py:80
  95.3 4.4 %fusion.82 = f32[32,8192]{1,0:T(8,128)} fusion(s32[512]{0:T(512)S(1)} %bitcast.74, f32[32,8192]{1,0:T(8,128)} %get-tuple-element.116, pred[]{:T(512)S(6)} %compare.3, bf16[4,32,512]{2,1,0:T(8,128)(2,1)S(1)} %get-tuple-element.123, s32[]{:T(128)} %get-tuple-element.115), kind=kOutput, calls=%fused_computation.3.clone.1 | convolution fusion | flops 273154048 | bytes 2131973 | tf_op jit(solution)/shard_map/while/body/eval_jaxpr/dot_general | solution.py:78
  99.7 5.6 %fusion.82 = f32[32,8192]{1,0:T(8,128)} fusion(s32[512]{0:T(512)S(1)} %bitcast.74, f32[32,8192]{1,0:T(8,128)} %get-tuple-element.116, pred[]{:T(512)S(6)} %compare.3, bf16[4,32,512]{2,1,0:T(8,128)(2,1)S(1)} %get-tuple-element.123, s32[]{:T(128)} %get-tuple-element.115), kind=kOutput, calls=%fused_computation.3.clone.1 | convolution fusion | flops 273154048 | bytes 2131973 | tf_op jit(solution)/shard_map/while/body/eval_jaxpr/dot_general | solution.py:78
  105.4 5.6 %fusion.82 = f32[32,8192]{1,0:T(8,128)} fusion(s32[512]{0:T(512)S(1)} %bitcast.74, f32[32,8192]{1,0:T(8,128)} %get-tuple-element.116, pred[]{:T(512)S(6)} %compare.3, bf16[4,32,512]{2,1,0:T(8,128)(2,1)S(1)} %get-tuple-element.123, s32[]{:T(128)} %get-tuple-element.115), kind=kOutput, calls=%fused_computation.3.clone.1 | convolution fusion | flops 273154048 | bytes 2131973 | tf_op jit(solution)/shard_map/while/body/eval_jaxpr/dot_general | solution.py:78
  111.0 5.6 %fusion.82 = f32[32,8192]{1,0:T(8,128)} fusion(s32[512]{0:T(512)S(1)} %bitcast.74, f32[32,8192]{1,0:T(8,128)} %get-tuple-element.116, pred[]{:T(512)S(6)} %compare.3, bf16[4,32,512]{2,1,0:T(8,128)(2,1)S(1)} %get-tuple-element.123, s32[]{:T(128)} %get-tuple-element.115), kind=kOutput, calls=%fused_computation.3.clone.1 | convolution fusion | flops 273154048 | bytes 2131973 | tf_op jit(solution)/shard_map/while/body/eval_jaxpr/dot_general | solution.py:78
  116.6 2.5 %copy.45 = f32[4,8,32,256]{3,2,1,0:T(8,128)} copy(f32[4,8,32,256]{3,1,2,0:T(8,128)} %bitcast.71) | data formatting | bytes 2097152
  119.1 1.6 %copy.38 = f32[2,32,34,1]{3,2,1,0:T(8,128)} copy(f32[2,32,34,1]{2,1,3,0:T(8,128)S(1)} %collective-permute-done.10) | data formatting | bytes 17408 | tf_op jit(solution)/shard_map/ppermute | solution.py:19
  120.8 1.6 %copy.39 = f32[2,32,34,1]{3,2,1,0:T(8,128)} copy(f32[2,32,34,1]{2,1,3,0:T(8,128)S(1)} %collective-permute-done.11) | data formatting | bytes 17408 | tf_op jit(solution)/shard_map/ppermute | solution.py:20
  122.4 4.4 %fusion.19 = f32[2,32,34,258]{3,2,1,0:T(8,128)S(1)} fusion(f32[1,32,32,256]{3,2,1,0:T(8,128)S(1)} %bitcast.57, f32[2,32,34,1]{3,2,1,0:T(8,128)} %copy.39, f32[2,32,1,256]{3,2,1,0:T(1,128)S(1)} %collective-permute-done.9, f32[1,32,32,256]{3,2,1,0:T(8,128)} %bitcast.63, f32[2,32,1,256]{3,2,1,0:T(1,128)S(1)} %collective-permute-done.8, f32[2,32,34,1]{3,2,1,0:T(8,128)} %copy.38), kind=kLoop, calls=%fused_computation.23 | loop fusion | flops 2807040 | bytes 4491264 | tf_op jit(solution)/shard_map/concatenate | solution.py:21
  127.2 0.9 copy-done.4
  128.4 0.3 copy-done.9
  128.7 0.3 copy-done.10
  129.0 3.0 %bitcast_add_fusion = f32[32,32,256]{2,1,0:T(8,128)S(1)} fusion(f32[4,8,32,256]{3,2,1,0:T(8,128)S(1)} %copy-done.9, f32[32,32,256]{2,1,0:T(8,128)S(1)} %copy-done.4, f32[32,32,256]{2,1,0:T(8,128)S(1)} %copy-done.6, f32[32,34,258]{2,1,0:T(8,128)S(1)} %get-tuple-element.67, f32[32,32,256]{2,1,0:T(8,128)S(1)} %convert_select_fusion, ...), kind=kLoop, calls=%fused_computation.47 | loop fusion | flops 8126464 | bytes 18874368 | tf_op jit(solution)/shard_map/add | solution.py:84
  132.0 0.6 copy.41
  132.6 15.1 %all_to_all.24 = f32[32,32,256]{2,0,1:T(8,128)S(1)} all-to-all(f32[32,32,256]{2,0,1:T(8,128)S(1)} %copy.41), channel_id=1, replica_groups=mesh['cap'=4,'lat'=4,'rad'=2] {'rad'}, dimensions={1} | all-to-all | bytes 2097152 | tf_op jit(solution)/shard_map/all_to_all | solution.py:86
  147.7 0.6 copy.42
  148.4 0.6 copy.46
  149.0 1.1 fusion.76
  150.1 1.3 copy.47
  (43 shorter events, 1.6 us)
Async XLA Ops:
  0.0 149.0 %copy-start = (f32[64,64]{1,0:T(8,128)S(1)}, f32[64,64]{1,0:T(8,128)}, u32[]{:S(2)}) copy-start(f32[64,64]{1,0:T(8,128)} %param.16) | copy-start | bytes 49156
  0.0 1.9 %copy-start.1 = (f32[32,32,256]{2,1,0:T(8,128)S(1)}, f32[32,32,256]{2,1,0:T(8,128)}, u32[]{:S(2)}) copy-start(f32[32,32,256]{2,1,0:T(8,128)} %param.11) | copy-start | bytes 3145732
  2.1 5.4 %collective-permute-start = (f32[2,32,1,256]{3,2,1,0:T(1,128)S(1)}, f32[2,32,1,256]{3,2,1,0:T(1,128)S(1)}, u32[]{:S(2)}, u32[]{:S(2)}) collective-permute-start(f32[2,32,1,256]{3,2,1,0:T(1,128)S(1)} %get-tuple-element.62), channel_id=1, source_target_pairs={{0,8},{8,16},{16,24},{1,9},{9,17},{17,25},{2,10},{10,18},{18,26},{... | collective-permute-start | bytes 196616 | tf_op jit(solution)/shard_map/ppermute | solution.py:19
  6.1 5.0 %collective-permute-start.1 = (f32[2,32,1,256]{3,2,1,0:T(1,128)S(1)}, f32[2,32,1,256]{3,2,1,0:T(1,128)S(1)}, u32[]{:S(2)}, u32[]{:S(2)}) collective-permute-start(f32[2,32,1,256]{3,2,1,0:T(1,128)S(1)} %get-tuple-element.82), channel_id=1, source_target_pairs={{8,0},{16,8},{24,16},{9,1},{17,9},{25,17},{10,2},{18,10},{26,18},{... | collective-permute-start | bytes 196616 | tf_op jit(solution)/shard_map/ppermute | solution.py:20
  15.3 8.9 %collective-permute-start.2 = (f32[2,32,34,1]{2,1,3,0:T(8,128)S(1)}, f32[2,32,34,1]{2,1,3,0:T(8,128)S(1)}, u32[]{:S(2)}, u32[]{:S(2)}) collective-permute-start(f32[2,32,34,1]{2,1,3,0:T(8,128)S(1)} %copy.28), channel_id=1, source_target_pairs={{0,2},{2,4},{4,6},{1,3},{3,5},{5,7},{8,10},{10,12},{12,14},{9,11},... | collective-permute-start | bytes 26120 | tf_op jit(solution)/shard_map/ppermute | solution.py:19
  22.3 5.2 %collective-permute-start.3 = (f32[2,32,34,1]{2,1,3,0:T(8,128)S(1)}, f32[2,32,34,1]{2,1,3,0:T(8,128)S(1)}, u32[]{:S(2)}, u32[]{:S(2)}) collective-permute-start(f32[2,32,34,1]{2,1,3,0:T(8,128)S(1)} %copy.29), channel_id=1, source_target_pairs={{2,0},{4,2},{6,4},{3,1},{5,3},{7,5},{10,8},{12,10},{14,12},{11,9},... | collective-permute-start | bytes 26120 | tf_op jit(solution)/shard_map/ppermute | solution.py:20
  33.4 1.2 copy-start.2
  34.7 8.2 %copy-start.11 = (bf16[32,2048]{1,0:T(8,128)(2,1)S(1)}, bf16[32,2048]{1,0:T(8,128)(2,1)}, u32[]{:S(2)}) copy-start(bf16[32,2048]{1,0:T(8,128)(2,1)} %param.17) | copy-start | bytes 393220
  36.7 1.0 copy-start.7
  38.4 8.5 %collective-permute-start.4 = (f32[2,32,1,256]{3,2,1,0:T(1,128)}, f32[2,32,1,256]{3,2,1,0:T(1,128)S(1)}, u32[]{:S(2)}, u32[]{:S(2)}) collective-permute-start(f32[2,32,1,256]{3,2,1,0:T(1,128)} %get-tuple-element.80), channel_id=1, source_target_pairs={{0,8},{8,16},{16,24},{1,9},{9,17},{17,25},{2,10},{10,18},{18,26},{... | collective-permute-start | bytes 196616 | tf_op jit(solution)/shard_map/ppermute | solution.py:19
  41.6 5.3 %collective-permute-start.5 = (f32[2,32,1,256]{3,2,1,0:T(1,128)S(1)}, f32[2,32,1,256]{3,2,1,0:T(1,128)S(1)}, u32[]{:S(2)}, u32[]{:S(2)}) collective-permute-start(f32[2,32,1,256]{3,2,1,0:T(1,128)S(1)} %get-tuple-element.81), channel_id=1, source_target_pairs={{8,0},{16,8},{24,16},{9,1},{17,9},{25,17},{10,2},{18,10},{26,18},{... | collective-permute-start | bytes 196616 | tf_op jit(solution)/shard_map/ppermute | solution.py:20
  43.5 51.7 %all-to-all-start = ((bf16[32,4,512]{2,0,1:T(8,128)(2,1)}), bf16[32,4,512]{2,0,1:T(8,128)(2,1)S(1)}, u32[]{:S(2)}, u32[]{:S(2)}) async-start(bf16[32,4,512]{2,0,1:T(8,128)(2,1)} %bitcast.46), calls=%async_computation | async-start | bytes 262144 | tf_op jit(solution)/shard_map/all_to_all | solution.py:62
  50.4 9.0 %copy-start.13 = (s32[4]{0:T(128)S(1)}, s32[4]{0:T(128)}, u32[]{:S(2)}) copy-start(s32[4]{0:T(128)} %param.19) | copy-start | bytes 52
  52.2 7.2 %collective-permute-start.6 = (f32[2,32,34,1]{2,1,3,0:T(8,128)S(1)}, f32[2,32,34,1]{2,1,3,0:T(8,128)S(1)}, u32[]{:S(2)}, u32[]{:S(2)}) collective-permute-start(f32[2,32,34,1]{2,1,3,0:T(8,128)S(1)} %copy.32), channel_id=1, source_target_pairs={{0,2},{2,4},{4,6},{1,3},{3,5},{5,7},{8,10},{10,12},{12,14},{9,11},... | collective-permute-start | bytes 26120 | tf_op jit(solution)/shard_map/ppermute | solution.py:19
  57.2 5.3 %collective-permute-start.7 = (f32[2,32,34,1]{2,1,3,0:T(8,128)S(1)}, f32[2,32,34,1]{2,1,3,0:T(8,128)}, u32[]{:S(2)}, u32[]{:S(2)}) collective-permute-start(f32[2,32,34,1]{2,1,3,0:T(8,128)S(1)} %copy.33), channel_id=1, source_target_pairs={{2,0},{4,2},{6,4},{3,1},{5,3},{7,5},{10,8},{12,10},{14,12},{11,9},... | collective-permute-start | bytes 26120 | tf_op jit(solution)/shard_map/ppermute | solution.py:20
  69.4 1.2 copy-start.3
  69.4 1.5 %copy-start.8 = (f32[32,32,256]{2,1,0:T(8,128)S(1)}, f32[32,32,256]{2,1,0:T(8,128)}, u32[]{:S(2)}) copy-start(f32[32,32,256]{2,1,0:T(8,128)} %copy-done.7) | copy-start | bytes 3145732
  70.9 7.7 %copy-start.12 = (s32[2048]{0:T(1024)S(1)}, s32[2048]{0:T(1024)}, u32[]{:S(2)}) copy-start(s32[2048]{0:T(1024)} %param.18) | copy-start | bytes 24580
  72.8 1.0 copy-start.5
  73.9 4.8 %collective-permute-start.8 = (f32[2,32,1,256]{3,2,1,0:T(1,128)S(1)}, f32[2,32,1,256]{3,2,1,0:T(1,128)S(1)}, u32[]{:S(2)}, u32[]{:S(2)}) collective-permute-start(f32[2,32,1,256]{3,2,1,0:T(1,128)S(1)} %get-tuple-element.78), channel_id=1, source_target_pairs={{0,8},{8,16},{16,24},{1,9},{9,17},{17,25},{2,10},{10,18},{18,26},{... | collective-permute-start | bytes 196616 | tf_op jit(solution)/shard_map/ppermute | solution.py:19
  77.3 5.0 %collective-permute-start.9 = (f32[2,32,1,256]{3,2,1,0:T(1,128)S(1)}, f32[2,32,1,256]{3,2,1,0:T(1,128)S(1)}, u32[]{:S(2)}, u32[]{:S(2)}) collective-permute-start(f32[2,32,1,256]{3,2,1,0:T(1,128)S(1)} %get-tuple-element.79), channel_id=1, source_target_pairs={{8,0},{16,8},{24,16},{9,1},{17,9},{25,17},{10,2},{18,10},{26,18},{... | collective-permute-start | bytes 196616 | tf_op jit(solution)/shard_map/ppermute | solution.py:20
  87.7 31.5 %collective-permute-start.10 = (f32[2,32,34,1]{2,1,3,0:T(8,128)S(1)}, f32[2,32,34,1]{2,1,3,0:T(8,128)S(1)}, u32[]{:S(2)}, u32[]{:S(2)}) collective-permute-start(f32[2,32,34,1]{2,1,3,0:T(8,128)S(1)} %copy.36), channel_id=1, source_target_pairs={{0,2},{2,4},{4,6},{1,3},{3,5},{5,7},{8,10},{10,12},{12,14},{9,11},... | collective-permute-start | bytes 26120 | tf_op jit(solution)/shard_map/ppermute | solution.py:19
  93.1 27.7 %collective-permute-start.11 = (f32[2,32,34,1]{2,1,3,0:T(8,128)S(1)}, f32[2,32,34,1]{2,1,3,0:T(8,128)S(1)}, u32[]{:S(2)}, u32[]{:S(2)}) collective-permute-start(f32[2,32,34,1]{2,1,3,0:T(8,128)S(1)} %copy.37), channel_id=1, source_target_pairs={{2,0},{4,2},{6,4},{3,1},{5,3},{7,5},{10,8},{12,10},{14,12},{11,9},... | collective-permute-start | bytes 26120 | tf_op jit(solution)/shard_map/ppermute | solution.py:20
  126.8 1.2 copy-start.4
  126.9 1.5 %copy-start.6 = (f32[32,32,256]{2,1,0:T(8,128)S(1)}, f32[32,32,256]{2,1,0:T(8,128)}, u32[]{:S(2)}) copy-start(f32[32,32,256]{2,1,0:T(8,128)} %copy-done.5) | copy-start | bytes 3145732
  126.9 1.8 %copy-start.9 = (f32[4,8,32,256]{3,2,1,0:T(8,128)S(1)}, f32[4,8,32,256]{3,2,1,0:T(8,128)}, u32[]{:S(2)}) copy-start(f32[4,8,32,256]{3,2,1,0:T(8,128)} %copy.45) | copy-start | bytes 3145732
  126.9 2.1 %copy-start.10 = (bf16[2,32,32,256]{3,2,1,0:T(8,128)(2,1)S(1)}, bf16[2,32,32,256]{3,2,1,0:T(8,128)(2,1)}, u32[]{:S(2)}) copy-start(bf16[2,32,32,256]{3,2,1,0:T(8,128)(2,1)} %param.12) | copy-start | bytes 3145732
where the time goes:
time: 153 us; the launch traced here: 151 us
  local copies, waits for them, and re-layouts  40.6 us (27%)
  starting transfers between devices  35.8 us (23%)
  other arithmetic  26.6 us (17%)
  matrix products  22.4 us (15%)
  blocking collectives  15.1 us (10%)
  waiting for transfers between devices  10.5 us (7%)
    ppermute x6, starting transfers between devices, extended(): before = lax.ppermute(last, axis, up)  22.4 us
    dot_general x4, matrix products, deposit_block(): jnp.dot(rows_part, onehot, preferred_element_type=jnp.float32)  21.3 us
    concatenate x6, other arithmetic, extended(): x = jnp.concatenate([before, x, after], axis=dim)  16.7 us
    all_to_all x1, blocking collectives, per_device(): lax.all_to_all(rhs, 'rad', split_axis=1, concat_axis=0, tiled=True)  15.1 us
    slice x6, local copies, waits for them, and re-layouts, extended(): last = lax.slice_in_dim(x, length - width, length, axis=dim)  11.2 us
    ppermute x6, waiting for transfers between devices, extended(): after = lax.ppermute(first, axis, down)  10.5 us
    unnamed x32, local copies, waits for them, and re-layouts  10.5 us
    ppermute x6, starting transfers between devices, extended(): after = lax.ppermute(first, axis, down)  10 us
  transfers between devices with their start and end apart: 13, of which 4 were waited for; matrix products, arithmetic and copies ran while one was open for 36% of the time, Pallas kernels for 0%

commit v1 on v0

--- a/solution.py
+++ b/solution.py
@@ -83,7 +83,9 @@
     deposit = deposit.reshape(layers, first_len, second_len)
     rhs = iterate + advect_coef * advect + deposit
     full_layers = radial_inverse.shape[0]
-    columns = lax.all_to_all(rhs, "rad", split_axis=1, concat_axis=0, tiled=True)
+    columns = jnp.concatenate(
+        lax.all_to_all(jnp.stack(jnp.split(rhs, lax.axis_size("rad"), axis=1)), "rad", 0, 0), axis=0
+    )
     result = jnp.dot(
         radial_inverse, columns.reshape(full_layers, -1), precision=lax.Precision.HIGHEST
     )

time: 153 us -> 151 us (0.987)
  no operation moved by 1% of the time
where the time goes in v1:
time: 151 us; the launch traced here: 150 us
  local copies, waits for them, and re-layouts  39.4 us (26%)
  starting transfers between devices  35.8 us (24%)
  other arithmetic  26.6 us (18%)
  matrix products  22.4 us (15%)
  blocking collectives  15.1 us (10%)
  waiting for transfers between devices  10.5 us (7%)
    ppermute x6, starting transfers between devices, extended(): before = lax.ppermute(last, axis, up)  22.5 us
    dot_general x4, matrix products, deposit_block(): jnp.dot(rows_part, onehot, preferred_element_type=jnp.float32)  21.3 us
    concatenate x6, other arithmetic, extended(): x = jnp.concatenate([before, x, after], axis=dim)  16.7 us
    all_to_all x1, blocking collectives, per_device(): lax.all_to_all(jnp.stack(jnp.split(rhs, lax.axis_size('rad'), axis=1)), '...  15.1 us
    slice x6, local copies, waits for them, and re-layouts, extended(): last = lax.slice_in_dim(x, length - width, length, axis=dim)  11.2 us
    unnamed x32, local copies, waits for them, and re-layouts  10.5 us
    ppermute x6, waiting for transfers between devices, extended(): after = lax.ppermute(first, axis, down)  10.5 us
    ppermute x6, starting transfers between devices, extended(): after = lax.ppermute(first, axis, down)  10 us
  transfers between devices with their start and end apart: 13, of which 4 were waited for; matrix products, arithmetic and copies ran while one was open for 36% of the time, Pallas kernels for 0%

profile of v1, /device:TPU:1, one launch (start us, length us, event | category | flops | bytes accessed | tf_op | source)
XLA Modules:
  0.0 150.3 jit_solution(2071247404623888754)
XLA Ops:
  0.0 1.9 %convert_select_fusion = f32[32,32,256]{2,1,0:T(8,128)S(1)} fusion(bf16[32,32,256]{2,1,0:T(8,128)(2,1)} %param.13, bf16[32,32,256]{2,1,0:T(8,128)(2,1)} %param.14, s32[32,32,256]{2,1,0:T(8,128)} %param.15), kind=kLoop, calls=%fused_computation.43 | loop fusion | flops 1835008 | bytes 3145728 | tf_op jit(solution)/shard_map/jit(_where)/select_n | solution.py:51
  2.1 4.0 %collective-permute-start = (f32[2,32,1,256]{3,2,1,0:T(1,128)S(1)}, f32[2,32,1,256]{3,2,1,0:T(1,128)S(1)}, u32[]{:S(2)}, u32[]{:S(2)}) collective-permute-start(f32[2,32,1,256]{3,2,1,0:T(1,128)S(1)} %get-tuple-element.62), channel_id=1, source_target_pairs={{0,8},{8,16},{16,24},{1,9},{9,17},{17,25},{2,10},{10,18},{18,26},{... | collective-permute-start | bytes 196616 | tf_op jit(solution)/shard_map/ppermute | solution.py:19
  6.1 1.3 collective-permute-start.1
  7.4 3.7 %collective-permute-done.1 = f32[2,32,1,256]{3,2,1,0:T(1,128)S(1)} collective-permute-done((f32[2,32,1,256]{3,2,1,0:T(1,128)S(1)}, f32[2,32,1,256]{3,2,1,0:T(1,128)S(1)}, u32[]{:S(2)}, u32[]{:S(2)}) %collective-permute-start.1) | collective-permute-done | bytes 65568 | tf_op jit(solution)/shard_map/ppermute | solution.py:20
  11.1 0.4 fusion.21
  11.6 1.9 %fusion.75 = (f32[2,32,34,1]{3,2,1,0:T(8,128)}, f32[2,32,34,1]{3,2,1,0:T(8,128)}) fusion(f32[2,32,34,256]{3,2,1,0:T(8,128)S(1)} %fusion.21), kind=kLoop, calls=%fused_computation.127 | loop fusion | bytes 34816 | tf_op jit(solution)/shard_map/slice | solution.py:17
  13.5 1.9 %copy.25 = f32[2,32,34,1]{2,1,3,0:T(8,128)S(1)} copy(f32[2,32,34,1]{3,2,1,0:T(8,128)} %get-tuple-element.76) | data formatting | bytes 17408 | tf_op jit(solution)/shard_map/slice | solution.py:17
  15.3 5.1 %collective-permute-start.2 = (f32[2,32,34,1]{2,1,3,0:T(8,128)S(1)}, f32[2,32,34,1]{2,1,3,0:T(8,128)S(1)}, u32[]{:S(2)}, u32[]{:S(2)}) collective-permute-start(f32[2,32,34,1]{2,1,3,0:T(8,128)S(1)} %copy.25), channel_id=1, source_target_pairs={{0,2},{2,4},{4,6},{1,3},{3,5},{5,7},{8,10},{10,12},{12,14},{9,11},... | collective-permute-start | bytes 26120 | tf_op jit(solution)/shard_map/ppermute | solution.py:19
  20.4 1.9 %copy.26 = f32[2,32,34,1]{2,1,3,0:T(8,128)S(1)} copy(f32[2,32,34,1]{3,2,1,0:T(8,128)} %get-tuple-element.77) | data formatting | bytes 17408 | tf_op jit(solution)/shard_map/slice | solution.py:18
  22.3 1.9 %collective-permute-start.3 = (f32[2,32,34,1]{2,1,3,0:T(8,128)S(1)}, f32[2,32,34,1]{2,1,3,0:T(8,128)S(1)}, u32[]{:S(2)}, u32[]{:S(2)}) collective-permute-start(f32[2,32,34,1]{2,1,3,0:T(8,128)S(1)} %copy.26), channel_id=1, source_target_pairs={{2,0},{4,2},{6,4},{3,1},{5,3},{7,5},{10,8},{12,10},{14,12},{11,9},... | collective-permute-start | bytes 26120 | tf_op jit(solution)/shard_map/ppermute | solution.py:20
  24.2 1.7 %copy.27 = f32[2,32,34,1]{3,2,1,0:T(8,128)} copy(f32[2,32,34,1]{2,1,3,0:T(8,128)S(1)} %collective-permute-done.2) | data formatting | bytes 17408 | tf_op jit(solution)/shard_map/ppermute | solution.py:19
  25.9 1.6 %collective-permute-done.3 = f32[2,32,34,1]{2,1,3,0:T(8,128)S(1)} collective-permute-done((f32[2,32,34,1]{2,1,3,0:T(8,128)S(1)}, f32[2,32,34,1]{2,1,3,0:T(8,128)S(1)}, u32[]{:S(2)}, u32[]{:S(2)}) %collective-permute-start.3) | collective-permute-done | bytes 8736 | tf_op jit(solution)/shard_map/ppermute | solution.py:20
  27.5 1.6 %copy.28 = f32[2,32,34,1]{3,2,1,0:T(8,128)} copy(f32[2,32,34,1]{2,1,3,0:T(8,128)S(1)} %collective-permute-done.3) | data formatting | bytes 17408 | tf_op jit(solution)/shard_map/ppermute | solution.py:20
  29.2 4.3 %fusion.11 = f32[2,32,34,258]{3,2,1,0:T(8,128)S(1)} fusion(f32[1,32,32,256]{3,2,1,0:T(8,128)S(1)} %bitcast.55, f32[2,32,34,1]{3,2,1,0:T(8,128)} %copy.28, f32[2,32,1,256]{3,2,1,0:T(1,128)S(1)} %collective-permute-done.1, f32[1,32,32,256]{3,2,1,0:T(8,128)S(1)} %bitcast.62, f32[2,32,1,256]{3,2,1,0:T(1,128)S(1)} %collective-permute-done, f32[2,32,34,1]{3,2,1,0:T(8,128)} %copy.27), kind=kLoop, calls=%fused_computation.15 | loop fusion | flops 2807040 | bytes 4491264 | tf_op jit(solution)/shard_map/concatenate | solution.py:21
  33.4 0.3 slice_bitcast_fusion.4
  33.7 1.0 copy-done.2
  34.7 2.0 %fusion.58 = f32[32,32,256]{2,1,0:T(8,128)S(1)} fusion(f32[32,32,256]{2,1,0:T(8,128)S(1)} %copy-done.2, f32[32,32,256]{2,1,0:T(8,128)S(1)} %convert_select_fusion, f32[32,34,258]{2,1,0:T(8,128)S(1)} %get-tuple-element.71, f32[32,34,258]{2,1,0:T(8,128)S(1)} %get-tuple-element.70), kind=kLoop, calls=%fused_computation.96 | loop fusion | flops 5505024 | bytes 11534336 | tf_op jit(solution)/shard_map/add | solution.py:58
  36.7 1.0 copy-done.7
  37.6 0.8 fusion.70
  38.4 3.2 %collective-permute-start.4 = (f32[2,32,1,256]{3,2,1,0:T(1,128)}, f32[2,32,1,256]{3,2,1,0:T(1,128)S(1)}, u32[]{:S(2)}, u32[]{:S(2)}) collective-permute-start(f32[2,32,1,256]{3,2,1,0:T(1,128)} %get-tuple-element.82), channel_id=1, source_target_pairs={{0,8},{8,16},{16,24},{1,9},{9,17},{17,25},{2,10},{10,18},{18,26},{... | collective-permute-start | bytes 196616 | tf_op jit(solution)/shard_map/ppermute | solution.py:19
  41.6 1.3 collective-permute-start.5
  42.9 0.7 copy.44
  43.5 3.3 %all-to-all-start = ((bf16[32,4,512]{2,0,1:T(8,128)(2,1)}), bf16[32,4,512]{2,0,1:T(8,128)(2,1)S(1)}, u32[]{:S(2)}, u32[]{:S(2)}) async-start(bf16[32,4,512]{2,0,1:T(8,128)(2,1)} %bitcast.48), calls=%async_computation | async-start | bytes 262144 | tf_op jit(solution)/shard_map/all_to_all | solution.py:62
  46.9 1.6 %fusion.23 = f32[2,32,34,256]{3,2,1,0:T(8,128)S(1)} fusion(f32[1,32,32,256]{3,2,1,0:T(8,128)S(1)} %bitcast.56, f32[2,32,1,256]{3,2,1,0:T(1,128)S(1)} %collective-permute-done.5, f32[1,32,32,256]{3,2,1,0:T(8,128)} %bitcast.67, f32[2,32,1,256]{3,2,1,0:T(1,128)S(1)} %collective-permute-done.4), kind=kLoop, calls=%fused_computation.30 | loop fusion | flops 1671168 | bytes 4456448 | tf_op jit(solution)/shard_map/concatenate | solution.py:21
  48.5 1.9 %fusion.74 = (f32[2,32,34,1]{3,2,1,0:T(8,128)}, f32[2,32,34,1]{3,2,1,0:T(8,128)}) fusion(f32[2,32,34,256]{3,2,1,0:T(8,128)S(1)} %fusion.23), kind=kLoop, calls=%fused_computation.126 | loop fusion | bytes 34816 | tf_op jit(solution)/shard_map/slice | solution.py:17
  50.4 1.9 %copy.29 = f32[2,32,34,1]{2,1,3,0:T(8,128)S(1)} copy(f32[2,32,34,1]{3,2,1,0:T(8,128)} %get-tuple-element.74) | data formatting | bytes 17408 | tf_op jit(solution)/shard_map/slice | solution.py:17
  52.2 3.1 %collective-permute-start.6 = (f32[2,32,34,1]{2,1,3,0:T(8,128)S(1)}, f32[2,32,34,1]{2,1,3,0:T(8,128)S(1)}, u32[]{:S(2)}, u32[]{:S(2)}) collective-permute-start(f32[2,32,34,1]{2,1,3,0:T(8,128)S(1)} %copy.29), channel_id=1, source_target_pairs={{0,2},{2,4},{4,6},{1,3},{3,5},{5,7},{8,10},{10,12},{12,14},{9,11},... | collective-permute-start | bytes 26120 | tf_op jit(solution)/shard_map/ppermute | solution.py:19
  55.4 1.9 %copy.30 = f32[2,32,34,1]{2,1,3,0:T(8,128)S(1)} copy(f32[2,32,34,1]{3,2,1,0:T(8,128)} %get-tuple-element.75) | data formatting | bytes 17408 | tf_op jit(solution)/shard_map/slice | solution.py:18
  57.2 2.1 %collective-permute-start.7 = (f32[2,32,34,1]{2,1,3,0:T(8,128)S(1)}, f32[2,32,34,1]{2,1,3,0:T(8,128)}, u32[]{:S(2)}, u32[]{:S(2)}) collective-permute-start(f32[2,32,34,1]{2,1,3,0:T(8,128)S(1)} %copy.30), channel_id=1, source_target_pairs={{2,0},{4,2},{6,4},{3,1},{5,3},{7,5},{10,8},{12,10},{14,12},{11,9},... | collective-permute-start | bytes 26120 | tf_op jit(solution)/shard_map/ppermute | solution.py:20
  59.4 1.7 %copy.31 = f32[2,32,34,1]{3,2,1,0:T(8,128)} copy(f32[2,32,34,1]{2,1,3,0:T(8,128)S(1)} %collective-permute-done.6) | data formatting | bytes 17408 | tf_op jit(solution)/shard_map/ppermute | solution.py:19
  61.1 1.5 collective-permute-done.7
  62.6 2.4 %copy.32 = f32[2,32,34,1]{3,2,1,0:T(8,128)} copy(f32[2,32,34,1]{2,1,3,0:T(8,128)} %collective-permute-done.7) | data formatting | bytes 17408 | tf_op jit(solution)/shard_map/ppermute | solution.py:20
  64.9 4.4 %fusion.15 = f32[2,32,34,258]{3,2,1,0:T(8,128)S(1)} fusion(f32[1,32,32,256]{3,2,1,0:T(8,128)S(1)} %bitcast.57, f32[2,32,34,1]{3,2,1,0:T(8,128)} %copy.32, f32[2,32,1,256]{3,2,1,0:T(1,128)S(1)} %collective-permute-done.5, f32[1,32,32,256]{3,2,1,0:T(8,128)} %bitcast.68, f32[2,32,1,256]{3,2,1,0:T(1,128)S(1)} %collective-permute-done.4, f32[2,32,34,1]{3,2,1,0:T(8,128)} %copy.31), kind=kLoop, calls=%fused_computation.19 | loop fusion | flops 2807040 | bytes 4491264 | tf_op jit(solution)/shard_map/concatenate | solution.py:21
  69.7 0.9 copy-done.3
  70.6 0.3 copy-done.8
  70.9 1.9 %fusion.44 = f32[32,32,256]{2,1,0:T(8,128)S(1)} fusion(f32[32,32,256]{2,1,0:T(8,128)S(1)} %copy-done.3, f32[32,32,256]{2,1,0:T(8,128)S(1)} %copy-done.8, f32[32,34,258]{2,1,0:T(8,128)S(1)} %get-tuple-element.69, f32[32,32,256]{2,1,0:T(8,128)S(1)} %convert_select_fusion, f32[32,34,258]{2,1,0:T(8,128)S(1)} %get-tuple-element.68), kind=kLoop, calls=%fused_computation.74 | loop fusion | flops 5505024 | bytes 12582912 | tf_op jit(solution)/shard_map/add | solution.py:58
  72.8 1.0 copy-done.5
  73.9 3.4 %collective-permute-start.8 = (f32[2,32,1,256]{3,2,1,0:T(1,128)S(1)}, f32[2,32,1,256]{3,2,1,0:T(1,128)S(1)}, u32[]{:S(2)}, u32[]{:S(2)}) collective-permute-start(f32[2,32,1,256]{3,2,1,0:T(1,128)S(1)} %get-tuple-element.80), channel_id=1, source_target_pairs={{0,8},{8,16},{16,24},{1,9},{9,17},{17,25},{2,10},{10,18},{18,26},{... | collective-permute-start | bytes 196616 | tf_op jit(solution)/shard_map/ppermute | solution.py:19
  77.4 1.3 collective-permute-start.9
  78.7 3.7 %collective-permute-done.9 = f32[2,32,1,256]{3,2,1,0:T(1,128)S(1)} collective-permute-done((f32[2,32,1,256]{3,2,1,0:T(1,128)S(1)}, f32[2,32,1,256]{3,2,1,0:T(1,128)S(1)}, u32[]{:S(2)}, u32[]{:S(2)}) %collective-permute-start.9) | collective-permute-done | bytes 65568 | tf_op jit(solution)/shard_map/ppermute | solution.py:20
  82.4 1.6 %fusion.25 = f32[2,32,34,256]{3,2,1,0:T(8,128)S(1)} fusion(f32[1,32,32,256]{3,2,1,0:T(8,128)S(1)} %bitcast.58, f32[2,32,1,256]{3,2,1,0:T(1,128)S(1)} %collective-permute-done.9, f32[1,32,32,256]{3,2,1,0:T(8,128)} %bitcast.64, f32[2,32,1,256]{3,2,1,0:T(1,128)S(1)} %collective-permute-done.8), kind=kLoop, calls=%fused_computation.32 | loop fusion | flops 1671168 | bytes 4456448 | tf_op jit(solution)/shard_map/concatenate | solution.py:21
  84.0 1.9 %fusion.73 = (f32[2,32,34,1]{3,2,1,0:T(8,128)}, f32[2,32,34,1]{3,2,1,0:T(8,128)}) fusion(f32[2,32,34,256]{3,2,1,0:T(8,128)S(1)} %fusion.25), kind=kLoop, calls=%fused_computation.125 | loop fusion | bytes 34816 | tf_op jit(solution)/shard_map/slice | solution.py:17
  85.8 1.9 %copy.33 = f32[2,32,34,1]{2,1,3,0:T(8,128)S(1)} copy(f32[2,32,34,1]{3,2,1,0:T(8,128)} %get-tuple-element.72) | data formatting | bytes 17408 | tf_op jit(solution)/shard_map/slice | solution.py:17
  87.7 3.6 %collective-permute-start.10 = (f32[2,32,34,1]{2,1,3,0:T(8,128)S(1)}, f32[2,32,34,1]{2,1,3,0:T(8,128)S(1)}, u32[]{:S(2)}, u32[]{:S(2)}) collective-permute-start(f32[2,32,34,1]{2,1,3,0:T(8,128)S(1)} %copy.33), channel_id=1, source_target_pairs={{0,2},{2,4},{4,6},{1,3},{3,5},{5,7},{8,10},{10,12},{12,14},{9,11},... | collective-permute-start | bytes 26120 | tf_op jit(solution)/shard_map/ppermute | solution.py:19
  91.3 1.9 %copy.34 = f32[2,32,34,1]{2,1,3,0:T(8,128)S(1)} copy(f32[2,32,34,1]{3,2,1,0:T(8,128)} %get-tuple-element.73) | data formatting | bytes 17408 | tf_op jit(solution)/shard_map/slice | solution.py:18
  93.1 2.1 %collective-permute-start.11 = (f32[2,32,34,1]{2,1,3,0:T(8,128)S(1)}, f32[2,32,34,1]{2,1,3,0:T(8,128)S(1)}, u32[]{:S(2)}, u32[]{:S(2)}) collective-permute-start(f32[2,32,34,1]{2,1,3,0:T(8,128)S(1)} %copy.34), channel_id=1, source_target_pairs={{2,0},{4,2},{6,4},{3,1},{5,3},{7,5},{10,8},{12,10},{14,12},{11,9},... | collective-permute-start | bytes 26120 | tf_op jit(solution)/shard_map/ppermute | solution.py:20
  95.3 21.3 %while.11 = (s32[]{:T(128)}, f32[32,8192]{1,0:T(8,128)}, bf16[4,32,512]{2,1,0:T(8,128)(2,1)S(1)}, s32[4,512]{1,0:T(4,128)S(1)}, s32[]{:T(128)}, /*index=5*/s32[]{:T(128)}) while((s32[]{:T(128)}, f32[32,8192]{1,0:T(8,128)}, bf16[4,32,512]{2,1,0:T(8,128)(2,1)S(1)}, s32[4,512]{1,0:T(4,128)S(1)}, s32[]{:T(128)}, ...), condition=%wide.region_1.2_spmd.clone, body=%wide.region_0.1_spmd.clone.sunk | while | flops 273154048 | bytes 2136151 | solution.py:80
  95.3 4.4 %fusion.82 = f32[32,8192]{1,0:T(8,128)} fusion(s32[512]{0:T(512)S(1)} %bitcast.75, f32[32,8192]{1,0:T(8,128)} %get-tuple-element.118, pred[]{:T(512)S(6)} %compare.3, bf16[4,32,512]{2,1,0:T(8,128)(2,1)S(1)} %get-tuple-element.125, s32[]{:T(128)} %get-tuple-element.117), kind=kOutput, calls=%fused_computation.3.clone.1 | convolution fusion | flops 273154048 | bytes 2131973 | tf_op jit(solution)/shard_map/while/body/eval_jaxpr/dot_general | solution.py:78
  99.8 5.6 %fusion.82 = f32[32,8192]{1,0:T(8,128)} fusion(s32[512]{0:T(512)S(1)} %bitcast.75, f32[32,8192]{1,0:T(8,128)} %get-tuple-element.118, pred[]{:T(512)S(6)} %compare.3, bf16[4,32,512]{2,1,0:T(8,128)(2,1)S(1)} %get-tuple-element.125, s32[]{:T(128)} %get-tuple-element.117), kind=kOutput, calls=%fused_computation.3.clone.1 | convolution fusion | flops 273154048 | bytes 2131973 | tf_op jit(solution)/shard_map/while/body/eval_jaxpr/dot_general | solution.py:78
  105.4 5.6 %fusion.82 = f32[32,8192]{1,0:T(8,128)} fusion(s32[512]{0:T(512)S(1)} %bitcast.75, f32[32,8192]{1,0:T(8,128)} %get-tuple-element.118, pred[]{:T(512)S(6)} %compare.3, bf16[4,32,512]{2,1,0:T(8,128)(2,1)S(1)} %get-tuple-element.125, s32[]{:T(128)} %get-tuple-element.117), kind=kOutput, calls=%fused_computation.3.clone.1 | convolution fusion | flops 273154048 | bytes 2131973 | tf_op jit(solution)/shard_map/while/body/eval_jaxpr/dot_general | solution.py:78
  111.0 5.6 %fusion.82 = f32[32,8192]{1,0:T(8,128)} fusion(s32[512]{0:T(512)S(1)} %bitcast.75, f32[32,8192]{1,0:T(8,128)} %get-tuple-element.118, pred[]{:T(512)S(6)} %compare.3, bf16[4,32,512]{2,1,0:T(8,128)(2,1)S(1)} %get-tuple-element.125, s32[]{:T(128)} %get-tuple-element.117), kind=kOutput, calls=%fused_computation.3.clone.1 | convolution fusion | flops 273154048 | bytes 2131973 | tf_op jit(solution)/shard_map/while/body/eval_jaxpr/dot_general | solution.py:78
  116.6 2.5 %copy.40 = f32[4,8,32,256]{3,2,1,0:T(8,128)} copy(f32[4,8,32,256]{3,1,2,0:T(8,128)} %bitcast.72) | data formatting | bytes 2097152
  119.2 1.7 %copy.35 = f32[2,32,34,1]{3,2,1,0:T(8,128)} copy(f32[2,32,34,1]{2,1,3,0:T(8,128)S(1)} %collective-permute-done.10) | data formatting | bytes 17408 | tf_op jit(solution)/shard_map/ppermute | solution.py:19
  120.8 1.6 %copy.36 = f32[2,32,34,1]{3,2,1,0:T(8,128)} copy(f32[2,32,34,1]{2,1,3,0:T(8,128)S(1)} %collective-permute-done.11) | data formatting | bytes 17408 | tf_op jit(solution)/shard_map/ppermute | solution.py:20
  122.5 4.4 %fusion.19 = f32[2,32,34,258]{3,2,1,0:T(8,128)S(1)} fusion(f32[1,32,32,256]{3,2,1,0:T(8,128)S(1)} %bitcast.59, f32[2,32,34,1]{3,2,1,0:T(8,128)} %copy.36, f32[2,32,1,256]{3,2,1,0:T(1,128)S(1)} %collective-permute-done.9, f32[1,32,32,256]{3,2,1,0:T(8,128)} %bitcast.65, f32[2,32,1,256]{3,2,1,0:T(1,128)S(1)} %collective-permute-done.8, f32[2,32,34,1]{3,2,1,0:T(8,128)} %copy.35), kind=kLoop, calls=%fused_computation.23 | loop fusion | flops 2807040 | bytes 4491264 | tf_op jit(solution)/shard_map/concatenate | solution.py:21
  127.2 0.9 copy-done.4
  128.1 0.3 copy-done.6
  128.4 0.3 copy-done.9
  128.7 0.3 copy-done.10
  129.1 3.0 %bitcast_add_fusion = f32[32,32,256]{2,1,0:T(8,128)S(1)} fusion(f32[4,8,32,256]{3,2,1,0:T(8,128)S(1)} %copy-done.9, f32[32,32,256]{2,1,0:T(8,128)S(1)} %copy-done.4, f32[32,32,256]{2,1,0:T(8,128)S(1)} %copy-done.6, f32[32,34,258]{2,1,0:T(8,128)S(1)} %get-tuple-element.67, f32[32,32,256]{2,1,0:T(8,128)S(1)} %convert_select_fusion, ...), kind=kLoop, calls=%fused_computation.47 | loop fusion | flops 8126464 | bytes 18874368 | tf_op jit(solution)/shard_map/add | solution.py:84
  132.2 15.1 %all_to_all.14 = f32[2,32,16,256]{3,2,1,0:T(8,128)S(1)} all-to-all(f32[2,32,16,256]{3,2,1,0:T(8,128)S(1)} %pad_maximum_fusion.6), channel_id=1, replica_groups=mesh['cap'=4,'lat'=4,'rad'=2] {'rad'}, dimensions={0} | all-to-all | bytes 2097152 | tf_op jit(solution)/shard_map/all_to_all | solution.py:87
  147.3 0.6 copy.41
  147.9 1.1 fusion.76
  149.0 1.3 copy.42
  (43 shorter events, 1.1 us)
Async XLA Ops:
  0.0 147.9 %copy-start = (f32[64,64]{1,0:T(8,128)S(1)}, f32[64,64]{1,0:T(8,128)}, u32[]{:S(2)}) copy-start(f32[64,64]{1,0:T(8,128)} %param.16) | copy-start | bytes 49156
  0.0 1.9 %copy-start.1 = (f32[32,32,256]{2,1,0:T(8,128)S(1)}, f32[32,32,256]{2,1,0:T(8,128)}, u32[]{:S(2)}) copy-start(f32[32,32,256]{2,1,0:T(8,128)} %param.11) | copy-start | bytes 3145732
  2.1 5.4 %collective-permute-start = (f32[2,32,1,256]{3,2,1,0:T(1,128)S(1)}, f32[2,32,1,256]{3,2,1,0:T(1,128)S(1)}, u32[]{:S(2)}, u32[]{:S(2)}) collective-permute-start(f32[2,32,1,256]{3,2,1,0:T(1,128)S(1)} %get-tuple-element.62), channel_id=1, source_target_pairs={{0,8},{8,16},{16,24},{1,9},{9,17},{17,25},{2,10},{10,18},{18,26},{... | collective-permute-start | bytes 196616 | tf_op jit(solution)/shard_map/ppermute | solution.py:19
  6.1 5.0 %collective-permute-start.1 = (f32[2,32,1,256]{3,2,1,0:T(1,128)S(1)}, f32[2,32,1,256]{3,2,1,0:T(1,128)S(1)}, u32[]{:S(2)}, u32[]{:S(2)}) collective-permute-start(f32[2,32,1,256]{3,2,1,0:T(1,128)S(1)} %get-tuple-element.84), channel_id=1, source_target_pairs={{8,0},{16,8},{24,16},{9,1},{17,9},{25,17},{10,2},{18,10},{26,18},{... | collective-permute-start | bytes 196616 | tf_op jit(solution)/shard_map/ppermute | solution.py:20
  15.3 8.9 %collective-permute-start.2 = (f32[2,32,34,1]{2,1,3,0:T(8,128)S(1)}, f32[2,32,34,1]{2,1,3,0:T(8,128)S(1)}, u32[]{:S(2)}, u32[]{:S(2)}) collective-permute-start(f32[2,32,34,1]{2,1,3,0:T(8,128)S(1)} %copy.25), channel_id=1, source_target_pairs={{0,2},{2,4},{4,6},{1,3},{3,5},{5,7},{8,10},{10,12},{12,14},{9,11},... | collective-permute-start | bytes 26120 | tf_op jit(solution)/shard_map/ppermute | solution.py:19
  22.3 5.2 %collective-permute-start.3 = (f32[2,32,34,1]{2,1,3,0:T(8,128)S(1)}, f32[2,32,34,1]{2,1,3,0:T(8,128)S(1)}, u32[]{:S(2)}, u32[]{:S(2)}) collective-permute-start(f32[2,32,34,1]{2,1,3,0:T(8,128)S(1)} %copy.26), channel_id=1, source_target_pairs={{2,0},{4,2},{6,4},{3,1},{5,3},{7,5},{10,8},{12,10},{14,12},{11,9},... | collective-permute-start | bytes 26120 | tf_op jit(solution)/shard_map/ppermute | solution.py:20
  33.4 1.2 copy-start.2
  34.7 8.2 %copy-start.11 = (bf16[32,2048]{1,0:T(8,128)(2,1)S(1)}, bf16[32,2048]{1,0:T(8,128)(2,1)}, u32[]{:S(2)}) copy-start(bf16[32,2048]{1,0:T(8,128)(2,1)} %param.17) | copy-start | bytes 393220
  36.7 1.0 copy-start.7
  38.4 8.5 %collective-permute-start.4 = (f32[2,32,1,256]{3,2,1,0:T(1,128)}, f32[2,32,1,256]{3,2,1,0:T(1,128)S(1)}, u32[]{:S(2)}, u32[]{:S(2)}) collective-permute-start(f32[2,32,1,256]{3,2,1,0:T(1,128)} %get-tuple-element.82), channel_id=1, source_target_pairs={{0,8},{8,16},{16,24},{1,9},{9,17},{17,25},{2,10},{10,18},{18,26},{... | collective-permute-start | bytes 196616 | tf_op jit(solution)/shard_map/ppermute | solution.py:19
  41.6 5.3 %collective-permute-start.5 = (f32[2,32,1,256]{3,2,1,0:T(1,128)S(1)}, f32[2,32,1,256]{3,2,1,0:T(1,128)S(1)}, u32[]{:S(2)}, u32[]{:S(2)}) collective-permute-start(f32[2,32,1,256]{3,2,1,0:T(1,128)S(1)} %get-tuple-element.83), channel_id=1, source_target_pairs={{8,0},{16,8},{24,16},{9,1},{17,9},{25,17},{10,2},{18,10},{26,18},{... | collective-permute-start | bytes 196616 | tf_op jit(solution)/shard_map/ppermute | solution.py:20
  43.5 51.8 %all-to-all-start = ((bf16[32,4,512]{2,0,1:T(8,128)(2,1)}), bf16[32,4,512]{2,0,1:T(8,128)(2,1)S(1)}, u32[]{:S(2)}, u32[]{:S(2)}) async-start(bf16[32,4,512]{2,0,1:T(8,128)(2,1)} %bitcast.48), calls=%async_computation | async-start | bytes 262144 | tf_op jit(solution)/shard_map/all_to_all | solution.py:62
  50.4 9.0 %copy-start.13 = (s32[4]{0:T(128)S(1)}, s32[4]{0:T(128)}, u32[]{:S(2)}) copy-start(s32[4]{0:T(128)} %param.19) | copy-start | bytes 52
  52.2 7.2 %collective-permute-start.6 = (f32[2,32,34,1]{2,1,3,0:T(8,128)S(1)}, f32[2,32,34,1]{2,1,3,0:T(8,128)S(1)}, u32[]{:S(2)}, u32[]{:S(2)}) collective-permute-start(f32[2,32,34,1]{2,1,3,0:T(8,128)S(1)} %copy.29), channel_id=1, source_target_pairs={{0,2},{2,4},{4,6},{1,3},{3,5},{5,7},{8,10},{10,12},{12,14},{9,11},... | collective-permute-start | bytes 26120 | tf_op jit(solution)/shard_map/ppermute | solution.py:19
  57.2 5.3 %collective-permute-start.7 = (f32[2,32,34,1]{2,1,3,0:T(8,128)S(1)}, f32[2,32,34,1]{2,1,3,0:T(8,128)}, u32[]{:S(2)}, u32[]{:S(2)}) collective-permute-start(f32[2,32,34,1]{2,1,3,0:T(8,128)S(1)} %copy.30), channel_id=1, source_target_pairs={{2,0},{4,2},{6,4},{3,1},{5,3},{7,5},{10,8},{12,10},{14,12},{11,9},... | collective-permute-start | bytes 26120 | tf_op jit(solution)/shard_map/ppermute | solution.py:20
  69.4 1.2 copy-start.3
  69.4 1.5 %copy-start.8 = (f32[32,32,256]{2,1,0:T(8,128)S(1)}, f32[32,32,256]{2,1,0:T(8,128)}, u32[]{:S(2)}) copy-start(f32[32,32,256]{2,1,0:T(8,128)} %copy-done.7) | copy-start | bytes 3145732
  70.9 7.8 %copy-start.12 = (s32[2048]{0:T(1024)S(1)}, s32[2048]{0:T(1024)}, u32[]{:S(2)}) copy-start(s32[2048]{0:T(1024)} %param.18) | copy-start | bytes 24580
  72.8 1.0 copy-start.5
  73.9 4.8 %collective-permute-start.8 = (f32[2,32,1,256]{3,2,1,0:T(1,128)S(1)}, f32[2,32,1,256]{3,2,1,0:T(1,128)S(1)}, u32[]{:S(2)}, u32[]{:S(2)}) collective-permute-start(f32[2,32,1,256]{3,2,1,0:T(1,128)S(1)} %get-tuple-element.80), channel_id=1, source_target_pairs={{0,8},{8,16},{16,24},{1,9},{9,17},{17,25},{2,10},{10,18},{18,26},{... | collective-permute-start | bytes 196616 | tf_op jit(solution)/shard_map/ppermute | solution.py:19
  77.4 5.0 %collective-permute-start.9 = (f32[2,32,1,256]{3,2,1,0:T(1,128)S(1)}, f32[2,32,1,256]{3,2,1,0:T(1,128)S(1)}, u32[]{:S(2)}, u32[]{:S(2)}) collective-permute-start(f32[2,32,1,256]{3,2,1,0:T(1,128)S(1)} %get-tuple-element.81), channel_id=1, source_target_pairs={{8,0},{16,8},{24,16},{9,1},{17,9},{25,17},{10,2},{18,10},{26,18},{... | collective-permute-start | bytes 196616 | tf_op jit(solution)/shard_map/ppermute | solution.py:20
  87.7 31.5 %collective-permute-start.10 = (f32[2,32,34,1]{2,1,3,0:T(8,128)S(1)}, f32[2,32,34,1]{2,1,3,0:T(8,128)S(1)}, u32[]{:S(2)}, u32[]{:S(2)}) collective-permute-start(f32[2,32,34,1]{2,1,3,0:T(8,128)S(1)} %copy.33), channel_id=1, source_target_pairs={{0,2},{2,4},{4,6},{1,3},{3,5},{5,7},{8,10},{10,12},{12,14},{9,11},... | collective-permute-start | bytes 26120 | tf_op jit(solution)/shard_map/ppermute | solution.py:19
  93.1 27.7 %collective-permute-start.11 = (f32[2,32,34,1]{2,1,3,0:T(8,128)S(1)}, f32[2,32,34,1]{2,1,3,0:T(8,128)S(1)}, u32[]{:S(2)}, u32[]{:S(2)}) collective-permute-start(f32[2,32,34,1]{2,1,3,0:T(8,128)S(1)} %copy.34), channel_id=1, source_target_pairs={{2,0},{4,2},{6,4},{3,1},{5,3},{7,5},{10,8},{12,10},{14,12},{11,9},... | collective-permute-start | bytes 26120 | tf_op jit(solution)/shard_map/ppermute | solution.py:20
  126.9 1.2 copy-start.4
  126.9 1.5 %copy-start.6 = (f32[32,32,256]{2,1,0:T(8,128)S(1)}, f32[32,32,256]{2,1,0:T(8,128)}, u32[]{:S(2)}) copy-start(f32[32,32,256]{2,1,0:T(8,128)} %copy-done.5) | copy-start | bytes 3145732
  126.9 1.8 %copy-start.9 = (f32[4,8,32,256]{3,2,1,0:T(8,128)S(1)}, f32[4,8,32,256]{3,2,1,0:T(8,128)}, u32[]{:S(2)}) copy-start(f32[4,8,32,256]{3,2,1,0:T(8,128)} %copy.40) | copy-start | bytes 3145732
  126.9 2.1 %copy-start.10 = (bf16[2,32,32,256]{3,2,1,0:T(8,128)(2,1)S(1)}, bf16[2,32,32,256]{3,2,1,0:T(8,128)(2,1)}, u32[]{:S(2)}) copy-start(bf16[2,32,32,256]{3,2,1,0:T(8,128)(2,1)} %param.12) | copy-start | bytes 3145732
